TPU v7x, 32 devices: a whole 2x2x4 slice. The times are simulated.
32 devices in a mesh: row: 8 (over z, y), col: 4 (over x, core).
Axes of the slice: x: 2, y: 2, z: 4, core: 2. Of those that a mesh axis runs over, the one named last changes fastest.
Arguments:
- x_scan: float32 [16384, 256], P(('row', 'col')), may hold values from -6 to 6
- owner_slot: int32 [16384], P(('row', 'col')), may hold values from 0 to 16383, as said below
- weight: float32 [256, 256], replicated, may hold values from -0.375 to 0.375
- norm_gain: float32 [256], replicated, may hold values from 0.1 to 1.9
- tile_values: float32 [32, 8, 128, 128], P(('row', 'col')), may hold values from -0.375 to 0.375
- tile_coords: int32 [32, 8, 2], P(('row', 'col')), may hold values from 0 to 3
- counts: int32 [32, 3], P(('row', 'col')), may hold values from 2 to 128, as said below
- boundary_rows: int32 [32, 2, 128], P(('row', 'col')), may hold values from 0 to 511
- coupling: float32 [32, 2, 128, 128], P(('row', 'col')), may hold values from -0.5 to 0.5
- cotangent: float32 [16384, 256], P(('row', 'col')), may hold values from -6 to 6
Outputs:
- output: float32 [16384, 256], P(('row', 'col'))
- x_grad: float32 [16384, 256], P(('row', 'col'))
- weight_grad: float32 [256, 256], replicated
- gain_grad: float32 [256], replicated
Inputs may be any that keep to these rules, and one draw needn't show every extreme that they name: Each value appears once. The scan rows of one partition go to partition owner_slot // 512: exactly 32 of them to one partition, none to another, and 16 to each of the rest. `counts`: column 0 lies between 2 and 8 and equals 8 on some partition; every other column lies between 32 and 128 and equals 128 on some partition.
All inputs are finite; a program needn't handle non-finite values.
Results may differ from a plain program's by a relative error of at most 0.0003.
Values sent between devices are 32-bit elements; how exact they have to be, the bound alone decides.
No kernel may reach another device: no remote copies, remote signals or barrier semaphores. Data moves between devices by JAX's collectives and lax.ppermute only.
A program may use at most 64 MiB of HBM per device.

v0:
```python
import math
import jax
import jax.numpy as jnp
from jax import lax
from jax.sharding import PartitionSpec as P

BLOCK = 128
ROUNDS = 2
EPS = 1e-05
PRECISE = lax.Precision.HIGHEST


def swapped(array, axis, apart):
    return lax.ppermute(array, axis, [(i, i ^ 1 << apart) for i in range(lax.axis_size(axis))])


def layer_piece(aggregate, weight, norm_gain):
    inv_scale = lax.rsqrt(jnp.mean(aggregate * aggregate, axis=-1, keepdims=True) + EPS)
    normed = aggregate * inv_scale * norm_gain
    return jax.nn.silu(
        jnp.dot(normed, weight, precision=PRECISE, preferred_element_type=jnp.float32)
    )


def interior(hidden, tile_values, tile_coords, live_count, transpose):
    feat_count = hidden.shape[1]
    blocks = hidden.reshape(-1, BLOCK, feat_count)
    if transpose:
        source_col, target_col, form = (0, 1, "tji,tjf->tif")
    else:
        source_col, target_col, form = (1, 0, "tij,tjf->tif")
    live_mask = (jnp.arange(tile_values.shape[0]) < live_count).astype(jnp.float32)
    source = blocks[tile_coords[:, source_col]]
    product = jnp.einsum(form, tile_values * live_mask[:, None, None], source, precision=PRECISE)
    result = jnp.zeros_like(blocks).at[tile_coords[:, target_col]].add(product)
    return result.reshape(hidden.shape)


def boundary_forward(total, hidden, boundary_rows, coupling, counts):
    for round_index in range(ROUNDS):
        picked = boundary_rows[0, round_index]
        own_mask = (jnp.arange(BLOCK) < counts[0, 1 + round_index]).astype(jnp.float32)[:, None]
        outgoing = hidden[picked] * own_mask
        received = swapped(outgoing, "col", round_index)
        contrib = (
            jnp.dot(
                coupling[0, round_index],
                received,
                precision=PRECISE,
                preferred_element_type=jnp.float32,
            )
            * own_mask
        )
        total = total.at[picked].add(contrib)
    return total


def boundary_backward(total, grad_agg, boundary_rows, coupling, counts):
    for round_index in range(ROUNDS):
        picked = boundary_rows[0, round_index]
        own_mask = (jnp.arange(BLOCK) < counts[0, 1 + round_index]).astype(jnp.float32)[:, None]
        outgoing = grad_agg[picked] * own_mask
        carried = jnp.dot(
            coupling[0, round_index].T,
            outgoing,
            precision=PRECISE,
            preferred_element_type=jnp.float32,
        )
        received = swapped(carried, "col", round_index)
        total = total.at[picked].add(received * own_mask)
    return total


def on_device(
    x_scan,
    owner_slot,
    weight,
    norm_gain,
    tile_values,
    tile_coords,
    counts,
    boundary_rows,
    coupling,
    cotangent,
):
    row_count, feat_count = x_scan.shape
    grid_rows = lax.axis_size("row")
    grid_cols = lax.axis_size("col")
    devices = grid_rows * grid_cols
    capacity = 2 * row_count // devices
    target = owner_slot // row_count
    within = owner_slot % row_count
    sorting = jnp.argsort(target, stable=True)
    sorted_target = target[sorting]
    per_peer = jnp.sum(
        (target[:, None] == jnp.arange(devices, dtype=jnp.int32)[None, :]).astype(jnp.int32), axis=0
    )
    starts = jnp.cumsum(per_peer) - per_peer
    ranked = (
        jnp.zeros((row_count,), jnp.int32)
        .at[sorting]
        .set(jnp.arange(row_count, dtype=jnp.int32) - starts[sorted_target])
    )
    bucket = target * capacity + ranked
    outbox = jnp.zeros((devices * capacity, feat_count), jnp.float32).at[bucket].set(x_scan)
    places = jnp.full((devices * capacity,), row_count, jnp.int32).at[bucket].set(within)
    inbox, place_in = (
        lax.all_to_all(
            outbox.reshape(devices, capacity, feat_count),
            ("row", "col"),
            split_axis=0,
            concat_axis=0,
            tiled=True,
        ),
        lax.all_to_all(
            places.reshape(devices, capacity),
            ("row", "col"),
            split_axis=0,
            concat_axis=0,
            tiled=True,
        ),
    )
    inbox = inbox.reshape(-1, feat_count)
    place_in = place_in.reshape(-1)
    hidden = jnp.zeros((row_count, feat_count), jnp.float32).at[place_in].set(inbox, mode="drop")
    aggregate = hidden + interior(hidden, tile_values[0], tile_coords[0], counts[0, 0], False)
    aggregate = boundary_forward(aggregate, hidden, boundary_rows, coupling, counts)
    activation, pullback = jax.vjp(layer_piece, aggregate, weight, norm_gain)
    output = hidden + activation
    grad_agg, grad_weight, grad_gain = pullback(cotangent)
    weight_sum, gain_sum = lax.psum((grad_weight, grad_gain), ("row", "col"))
    grad_nodes = (
        cotangent
        + grad_agg
        + interior(grad_agg, tile_values[0], tile_coords[0], counts[0, 0], True)
    )
    grad_nodes = boundary_backward(grad_nodes, grad_agg, boundary_rows, coupling, counts)
    valid = (place_in < row_count).astype(jnp.float32)[:, None]
    reply = grad_nodes[jnp.minimum(place_in, row_count - 1)] * valid
    returned = lax.all_to_all(
        reply.reshape(devices, capacity, feat_count),
        ("row", "col"),
        split_axis=0,
        concat_axis=0,
        tiled=True,
    )
    x_grad = returned.reshape(-1, feat_count)[bucket]
    node_scale = 1.0 / math.sqrt(row_count * devices)
    return (output, x_grad, weight_sum * node_scale, gain_sum * node_scale)


def solution(mesh):
    in_specs = (
        P(("row", "col"), None),
        P(("row", "col")),
        P(),
        P(),
        P(("row", "col"), None, None, None),
        P(("row", "col"), None, None),
        P(("row", "col"), None),
        P(("row", "col"), None, None),
        P(("row", "col"), None, None, None),
        P(("row", "col"), None),
    )
    out_specs = (P(("row", "col"), None), P(("row", "col"), None), P(), P())
    return jax.shard_map(
        on_device, mesh=mesh, in_specs=in_specs, out_specs=out_specs, check_vma=False
    )
```

profile of v0, /device:TPU:0, one launch (start us, length us, event | category | flops | bytes accessed | tf_op | source)
XLA Modules:
  0.0 280.3 jit_solution(10291379477697038767)
XLA Ops:
  9.8 3.8 %sort.17 = (s32[512]{0:T(512)}, s32[512]{0:T(512)S(1)}) sort(s32[512]{0:T(512)S(1)} %get-tuple-element.38, s32[512]{0:T(512)S(1)} %iota.29), dimensions={0}, to_apply=%region_0.1 | sort | flops 4608 | bytes 8192 | tf_op jit(solution)/shard_map/jit(argsort)/sort | solution.py:93
  13.5 3.5 %gather_fusion = s32[512]{0:T(512)S(1)} fusion(s32[512]{0:T(512)S(1)} %get-tuple-element.38, s32[1024]{0:T(1024)S(1)} %pad_clamp_fusion.5), kind=kCustom, calls=%fused_computation | custom fusion | bytes 6144 | tf_op jit(solution)/shard_map/gather | solution.py:94
  17.0 4.3 %compare_select_fusion.3 = (s32[512,1]{0,1:T(1,128)S(1)}, s32[512,1]{0,1:T(1,128)S(1)}) fusion(s32[]{:T(128)} %bitcast.27, s32[]{:T(128)} %bitcast.28, s32[]{:T(128)} %bitcast.29, s32[]{:T(128)} %bitcast.30, s32[]{:T(128)} %bitcast.31, s32[]{:T(128)} %bitcast.33, s32[]{:T(128)} %bitcast.32, s32[512,1]{0,1:T(1,128)S(1)} %bitcast.100), kind=kLoop, calls=%fused_computation.104 | loop fusion | flops 7680 | bytes 6172 | tf_op jit(solution)/shard_map/gather | solution.py:102
  21.5 15.8 %select_subtract_fusion = s32[512]{0:T(512)S(1)} fusion(pred[512]{0:T(512)(128)(4,1)S(1)} %get-tuple-element.32, pred[512]{0:T(512)(128)(4,1)S(1)} %get-tuple-element.31, pred[512]{0:T(512)(128)(4,1)S(1)} %get-tuple-element.30, pred[512]{0:T(512)(128)(4,1)S(1)} %get-tuple-element.29, pred[512]{0:T(512)(128)(4,1)S(1)} %get-tuple-element.28, ...), kind=kLoop, calls=%fused_computation.128 | loop fusion | flops 13312 | bytes 16996 | tf_op jit(solution)/shard_map/sub | solution.py:102
  37.3 2.4 scatter_custom_fusion
  39.7 2.4 scatter_custom_fusion.1
  42.9 7.3 %all-to-all-start = ((s32[32,1,32]{2,1,0:T(1,128)}), s32[32,1,32]{2,1,0:T(1,128)S(1)}, u32[]{:S(2)}, u32[]{:S(2)}) async-start(s32[32,1,32]{2,1,0:T(1,128)} %all_to_all.12), calls=%async_computation | async-start | bytes 32768 | tf_op jit(solution)/shard_map/all_to_all | solution.py:115
  50.2 3.7 %scatter_custom_fusion.2 = f32[1024,256]{1,0:T(8,128)} fusion(s32[512]{0:T(512)S(1)} %compare_select_fusion.9, f32[512,256]{1,0:T(8,128)} %param.10, f32[]{:T(128)} %constant.21.clone.1), kind=kCustom, calls=%fused_computation.38 | custom fusion | bytes 1049088 | tf_op jit(solution)/shard_map/scatter | solution.py:105
  53.9 3.3 %all-to-all-done = s32[32,1,32]{2,1,0:T(1,128)S(1)} async-done(((s32[32,1,32]{2,1,0:T(1,128)}), s32[32,1,32]{2,1,0:T(1,128)S(1)}, u32[]{:S(2)}, u32[]{:S(2)}) %all-to-all-start) | async-done | bytes 4128 | tf_op jit(solution)/shard_map/all_to_all | solution.py:115
  57.3 2.8 all-to-all-start.1
  65.3 20.9 %all-to-all-done.1 = f32[32,32,256]{2,1,0:T(8,128)S(1)} async-done(((f32[32,32,256]{2,1,0:T(8,128)}), f32[32,32,256]{2,1,0:T(8,128)S(1)}, u32[]{:S(2)}, u32[]{:S(2)}) %all-to-all-start.1) | async-done | bytes 1048608 | tf_op jit(solution)/shard_map/all_to_all | solution.py:108
  86.3 4.9 %scatter_custom_fusion.3 = f32[512,256]{1,0:T(8,128)S(1)} fusion(s32[1024]{0:T(1024)S(1)} %bitcast.101, f32[1024,256]{1,0:T(8,128)S(1)} %bitcast.96, f32[]{:T(128)} %constant.21.clone.1), kind=kCustom, calls=%fused_computation.54 | custom fusion | bytes 524292 | tf_op jit(solution)/shard_map/scatter | solution.py:125
  98.5 4.0 %collective-permute-done.1 = f32[128,256]{0,1:T(8,128)S(1)} collective-permute-done((f32[128,256]{0,1:T(8,128)S(1)}, f32[128,256]{0,1:T(8,128)S(1)}, u32[]{:S(2)}, u32[]{:S(2)}) %collective-permute-start.1) | collective-permute-done | bytes 131104 | tf_op jit(solution)/shard_map/ppermute | solution.py:14
  102.9 1.7 scatter_fusion.1
  112.1 2.1 fusion.6
  114.2 2.5 scatter_fusion.3
  119.3 4.3 %collective-permute-done.3 = f32[128,256]{0,1:T(8,128)S(1)} collective-permute-done((f32[128,256]{0,1:T(8,128)S(1)}, f32[128,256]{0,1:T(8,128)S(1)}, u32[]{:S(2)}, u32[]{:S(2)}) %collective-permute-start.3) | collective-permute-done | bytes 131104 | tf_op jit(solution)/shard_map/ppermute | solution.py:14
  126.7 3.5 %gather_fusion.7 = f32[1024,256]{1,0:T(8,128)S(1)} fusion(f32[512,256]{1,0:T(8,128)S(1)} %scatter_fusion.5, s32[1024]{0:T(1024)S(1)} %broadcast_clamp_fusion), kind=kCustom, calls=%fused_computation.7 | custom fusion | bytes 2101248 | tf_op jit(solution)/shard_map/gather | solution.py:139
  131.4 3.5 %all-to-all-start.2 = ((f32[32,32,256]{2,1,0:T(8,128)}), f32[32,32,256]{2,1,0:T(8,128)S(1)}, u32[]{:S(2)}, u32[]{:S(2)}) async-start(f32[32,32,256]{2,1,0:T(8,128)} %broadcast_multiply_fusion), calls=%async_computation.2 | async-start | bytes 2097152 | tf_op jit(solution)/shard_map/all_to_all | solution.py:140
  135.0 1.9 fusion.8
  136.9 45.2 %psum.15 = f32[256]{0:T(256)S(1)} all-reduce(f32[256]{0:T(256)S(1)} %get-tuple-element.6), channel_id=1, replica_groups=mesh['row'=8,'col'=4] {'row','col'}, use_global_device_ids=true, to_apply=%region_17.18 | all-reduce | flops 256 | bytes 2048 | tf_op jit(solution)/shard_map/psum | solution.py:131
  182.6 86.9 %all-reduce.2.cloned.1.call-done = f32[256,256]{1,0:T(8,128)} async-done(((f32[256,256]{1,0:T(8,128)}), f32[256,256]{1,0:T(8,128)}) %all-reduce.2.cloned.1.call-update) | async-done | bytes 262160 | tf_op jit(solution)/shard_map/psum | solution.py:131
  269.5 1.7 broadcast_multiply_fusion.1
  271.2 2.2 gather_fusion.8
  (101 shorter events, 31.1 us)
Async XLA Ops:
  7.2 99.1 %copy-start = (f32[256,256]{1,0:T(8,128)S(1)}, f32[256,256]{1,0:T(8,128)}, u32[]{:S(2)}) copy-start(f32[256,256]{1,0:T(8,128)} %param.12) | copy-start | bytes 786436
  42.9 14.4 %all-to-all-start = ((s32[32,1,32]{2,1,0:T(1,128)}), s32[32,1,32]{2,1,0:T(1,128)S(1)}, u32[]{:S(2)}, u32[]{:S(2)}) async-start(s32[32,1,32]{2,1,0:T(1,128)} %all_to_all.12), calls=%async_computation | async-start | bytes 32768 | tf_op jit(solution)/shard_map/all_to_all | solution.py:115
  57.2 2.8 copy-start.6
  57.3 29.0 %all-to-all-start.1 = ((f32[32,32,256]{2,1,0:T(8,128)}), f32[32,32,256]{2,1,0:T(8,128)S(1)}, u32[]{:S(2)}, u32[]{:S(2)}) async-start(f32[32,32,256]{2,1,0:T(8,128)} %bitcast.36), calls=%async_computation.1 | async-start | bytes 2097152 | tf_op jit(solution)/shard_map/all_to_all | solution.py:108
  62.6 0.7 copy-start.7
  63.3 0.7 copy-start.8
  91.2 1.0 copy-start.1
  95.6 2.5 collective-permute-start
  96.6 1.6 copy-start.3
  96.6 6.0 %collective-permute-start.1 = (f32[128,256]{0,1:T(8,128)S(1)}, f32[128,256]{0,1:T(8,128)S(1)}, u32[]{:S(2)}, u32[]{:S(2)}) collective-permute-start(f32[128,256]{0,1:T(8,128)S(1)} %broadcast_multiply_fusion.3), channel_id=1, source_target_pairs={{0,2},{1,3},{2,0},{3,1},{4,6},{5,7},{6,4},{7,5},{8,10},{9,11},{10,... | collective-permute-start | bytes 393224 | tf_op jit(solution)/shard_map/ppermute | solution.py:14
  106.3 0.7 copy-start.9
  107.0 1.5 copy-start.4
  108.4 0.9 copy-start.10
  111.0 1.0 copy-start.2
  114.2 2.5 copy-start.5
  117.2 2.0 collective-permute-start.2
  117.6 6.0 %collective-permute-start.3 = (f32[128,256]{0,1:T(8,128)S(1)}, f32[128,256]{0,1:T(8,128)S(1)}, u32[]{:S(2)}, u32[]{:S(2)}) collective-permute-start(f32[128,256]{0,1:T(8,128)S(1)} %convolution_bitcast_fusion), channel_id=1, source_target_pairs={{0,2},{1,3},{2,0},{3,1},{4,6},{5,7},{6,4},{7,5},{8,10},{9,11},{10,... | collective-permute-start | bytes 393224 | tf_op jit(solution)/shard_map/ppermute | solution.py:14
  131.4 3.6 %copy-start.11 = (f32[512,256]{1,0:T(8,128)S(1)}, f32[512,256]{1,0:T(8,128)}, u32[]{:S(2)}) copy-start(f32[512,256]{1,0:T(8,128)} %copy-done.10) | copy-start | bytes 1572868
  131.4 139.8 %all-to-all-start.2 = ((f32[32,32,256]{2,1,0:T(8,128)}), f32[32,32,256]{2,1,0:T(8,128)S(1)}, u32[]{:S(2)}, u32[]{:S(2)}) async-start(f32[32,32,256]{2,1,0:T(8,128)} %broadcast_multiply_fusion), calls=%async_computation.2 | async-start | bytes 2097152 | tf_op jit(solution)/shard_map/all_to_all | solution.py:140
  134.9 134.6 %all-reduce.2.cloned.1.call-start = ((), (), s32[]{:S(2)}) async-start(), calls=%async_computation.3 | async-start | bytes 524288 | tf_op jit(solution)/shard_map/psum | solution.py:131
Sparse Core Ops, SparseCore 0:
  141.9 127.6 all-reduce.1
where the time goes:
time: 281 us; the launch traced here: 280 us
  waiting for transfers between devices  119 us (42%)
  blocking collectives  45.2 us (16%)
  other arithmetic  41.7 us (15%)
  local copies, waits for them, and re-layouts  34 us (12%)
  starting transfers between devices  16.9 us (6%)
  between operations  14.6 us (5%)
  matrix products  8.46 us (3%)
    psum x1, waiting for transfers between devices, on_device(): weight_sum, gain_sum = lax.psum((grad_weight, grad_gain), ('row', 'col'))  86.9 us
    psum x1, blocking collectives, on_device(): weight_sum, gain_sum = lax.psum((grad_weight, grad_gain), ('row', 'col'))  45.2 us
    all_to_all x1, waiting for transfers between devices, on_device(): lax.all_to_all(outbox.reshape(devices, capacity, feat_count), ('row', 'co...  20.9 us
    sub x1, other arithmetic, on_device(): jnp.arange(row_count, dtype=jnp.int32) - starts[sorted_target]  15.8 us
    ppermute x4, waiting for transfers between devices, swapped(): lax.ppermute(array, axis, [(i, i ^ 1 << apart) for i in range(lax.axis_si...  8.32 us
    all_to_all x1, starting transfers between devices, on_device(): lax.all_to_all(places.reshape(devices, capacity), ('row', 'col'), split_a...  7.3 us
  transfers between devices with their start and end apart: 8, of which 5 were waited for; matrix products, arithmetic and copies ran while one was open for 5% of the time, Pallas kernels for 0%

commit v1 on v0

--- a/solution.py
+++ b/solution.py
@@ -128,7 +128,7 @@
     activation, pullback = jax.vjp(layer_piece, aggregate, weight, norm_gain)
     output = hidden + activation
     grad_agg, grad_weight, grad_gain = pullback(cotangent)
-    weight_sum, gain_sum = lax.psum((grad_weight, grad_gain), ("row", "col"))
+    weight_sum, gain_sum = lax.psum(lax.psum((grad_weight, grad_gain), "col"), "row")
     grad_nodes = (
         cotangent
         + grad_agg

time: 281 us -> 258 us (0.918)
  blocking collectives: 45.2 us -> 27.1 us
  waiting for transfers between devices: 119 us -> 114 us
    psum x1 -> x2, blocking collectives: 45.2 us -> 27.1 us  [the longest x1 21.4 us: on_device(): lax.psum(lax.psum((grad_weight, grad_gain), 'col'), 'row')]
    psum x1 -> x2, waiting for transfers between devices: 86.9 us -> 81.8 us  [the longest x1 46.6 us: on_device(): lax.psum(lax.psum((grad_weight, grad_gain), 'col'), 'row')]
  transfers between devices with their start and end apart: 8 -> 9, of which waited for: 5 -> 6; matrix products, arithmetic and copies ran while one was open for 5% -> 5% of each run, Pallas kernels for 0% -> 0%
where the time goes in v1:
time: 258 us; the launch traced here: 257 us
  waiting for transfers between devices  114 us (44%)
  other arithmetic  41.7 us (16%)
  local copies, waits for them, and re-layouts  34 us (13%)
  blocking collectives  27.1 us (11%)
  starting transfers between devices  16.9 us (7%)
  between operations  14.6 us (6%)
  matrix products  8.45 us (3%)
    psum x1, waiting for transfers between devices, on_device(): lax.psum(lax.psum((grad_weight, grad_gain), 'col'), 'row')  46.6 us
    psum x1, waiting for transfers between devices, on_device(): lax.psum((grad_weight, grad_gain), 'col')  35.2 us
    psum x1, blocking collectives, on_device(): lax.psum(lax.psum((grad_weight, grad_gain), 'col'), 'row')  21.4 us
    all_to_all x1, waiting for transfers between devices, on_device(): lax.all_to_all(outbox.reshape(devices, capacity, feat_count), ('row', 'co...  20.9 us
    sub x1, other arithmetic, on_device(): jnp.arange(row_count, dtype=jnp.int32) - starts[sorted_target]  15.8 us
    ppermute x4, waiting for transfers between devices, swapped(): lax.ppermute(array, axis, [(i, i ^ 1 << apart) for i in range(lax.axis_si...  8.31 us
    all_to_all x1, starting transfers between devices, on_device(): lax.all_to_all(places.reshape(devices, capacity), ('row', 'col'), split_a...  7.3 us
    psum x1, blocking collectives, on_device(): lax.psum((grad_weight, grad_gain), 'col')  5.76 us
  transfers between devices with their start and end apart: 9, of which 6 were waited for; matrix products, arithmetic and copies ran while one was open for 5% of the time, Pallas kernels for 0%

profile of v1, /device:TPU:0, one launch (start us, length us, event | category | flops | bytes accessed | tf_op | source)
XLA Modules:
  0.0 257.2 jit_solution(15490960518410638754)
XLA Ops:
  9.8 3.8 %sort.17 = (s32[512]{0:T(512)}, s32[512]{0:T(512)S(1)}) sort(s32[512]{0:T(512)S(1)} %get-tuple-element.38, s32[512]{0:T(512)S(1)} %iota.29), dimensions={0}, to_apply=%region_0.1 | sort | flops 4608 | bytes 8192 | tf_op jit(solution)/shard_map/jit(argsort)/sort | solution.py:93
  13.5 3.5 %gather_fusion = s32[512]{0:T(512)S(1)} fusion(s32[512]{0:T(512)S(1)} %get-tuple-element.38, s32[1024]{0:T(1024)S(1)} %pad_clamp_fusion.5), kind=kCustom, calls=%fused_computation | custom fusion | bytes 6144 | tf_op jit(solution)/shard_map/gather | solution.py:94
  17.0 4.3 %compare_select_fusion.3 = (s32[512,1]{0,1:T(1,128)S(1)}, s32[512,1]{0,1:T(1,128)S(1)}) fusion(s32[]{:T(128)} %bitcast.27, s32[]{:T(128)} %bitcast.28, s32[]{:T(128)} %bitcast.29, s32[]{:T(128)} %bitcast.30, s32[]{:T(128)} %bitcast.31, s32[]{:T(128)} %bitcast.33, s32[]{:T(128)} %bitcast.32, s32[512,1]{0,1:T(1,128)S(1)} %bitcast.100), kind=kLoop, calls=%fused_computation.104 | loop fusion | flops 7680 | bytes 6172 | tf_op jit(solution)/shard_map/gather | solution.py:102
  21.5 15.8 %select_subtract_fusion = s32[512]{0:T(512)S(1)} fusion(pred[512]{0:T(512)(128)(4,1)S(1)} %get-tuple-element.32, pred[512]{0:T(512)(128)(4,1)S(1)} %get-tuple-element.31, pred[512]{0:T(512)(128)(4,1)S(1)} %get-tuple-element.30, pred[512]{0:T(512)(128)(4,1)S(1)} %get-tuple-element.29, pred[512]{0:T(512)(128)(4,1)S(1)} %get-tuple-element.28, ...), kind=kLoop, calls=%fused_computation.128 | loop fusion | flops 13312 | bytes 16996 | tf_op jit(solution)/shard_map/sub | solution.py:102
  37.3 2.4 scatter_custom_fusion
  39.7 2.4 scatter_custom_fusion.1
  42.9 7.3 %all-to-all-start = ((s32[32,1,32]{2,1,0:T(1,128)}), s32[32,1,32]{2,1,0:T(1,128)S(1)}, u32[]{:S(2)}, u32[]{:S(2)}) async-start(s32[32,1,32]{2,1,0:T(1,128)} %all_to_all.12), calls=%async_computation | async-start | bytes 32768 | tf_op jit(solution)/shard_map/all_to_all | solution.py:115
  50.2 3.7 %scatter_custom_fusion.2 = f32[1024,256]{1,0:T(8,128)} fusion(s32[512]{0:T(512)S(1)} %compare_select_fusion.9, f32[512,256]{1,0:T(8,128)} %param.10, f32[]{:T(128)} %constant.21.clone.1), kind=kCustom, calls=%fused_computation.38 | custom fusion | bytes 1049088 | tf_op jit(solution)/shard_map/scatter | solution.py:105
  53.9 3.3 %all-to-all-done = s32[32,1,32]{2,1,0:T(1,128)S(1)} async-done(((s32[32,1,32]{2,1,0:T(1,128)}), s32[32,1,32]{2,1,0:T(1,128)S(1)}, u32[]{:S(2)}, u32[]{:S(2)}) %all-to-all-start) | async-done | bytes 4128 | tf_op jit(solution)/shard_map/all_to_all | solution.py:115
  57.3 2.8 %all-to-all-start.1 = ((f32[32,32,256]{2,1,0:T(8,128)}), f32[32,32,256]{2,1,0:T(8,128)S(1)}, u32[]{:S(2)}, u32[]{:S(2)}) async-start(f32[32,32,256]{2,1,0:T(8,128)} %bitcast.36), calls=%async_computation.1 | async-start | bytes 2097152 | tf_op jit(solution)/shard_map/all_to_all | solution.py:108
  65.3 20.9 %all-to-all-done.1 = f32[32,32,256]{2,1,0:T(8,128)S(1)} async-done(((f32[32,32,256]{2,1,0:T(8,128)}), f32[32,32,256]{2,1,0:T(8,128)S(1)}, u32[]{:S(2)}, u32[]{:S(2)}) %all-to-all-start.1) | async-done | bytes 1048608 | tf_op jit(solution)/shard_map/all_to_all | solution.py:108
  86.3 4.9 %scatter_custom_fusion.3 = f32[512,256]{1,0:T(8,128)S(1)} fusion(s32[1024]{0:T(1024)S(1)} %bitcast.101, f32[1024,256]{1,0:T(8,128)S(1)} %bitcast.96, f32[]{:T(128)} %constant.21.clone.1), kind=kCustom, calls=%fused_computation.54 | custom fusion | bytes 524292 | tf_op jit(solution)/shard_map/scatter | solution.py:125
  98.5 4.0 %collective-permute-done.1 = f32[128,256]{0,1:T(8,128)S(1)} collective-permute-done((f32[128,256]{0,1:T(8,128)S(1)}, f32[128,256]{0,1:T(8,128)S(1)}, u32[]{:S(2)}, u32[]{:S(2)}) %collective-permute-start.1) | collective-permute-done | bytes 131104 | tf_op jit(solution)/shard_map/ppermute | solution.py:14
  112.1 2.1 fusion.6
  114.2 2.5 scatter_fusion.3
  119.3 4.3 %collective-permute-done.3 = f32[128,256]{0,1:T(8,128)S(1)} collective-permute-done((f32[128,256]{0,1:T(8,128)S(1)}, f32[128,256]{0,1:T(8,128)S(1)}, u32[]{:S(2)}, u32[]{:S(2)}) %collective-permute-start.3) | collective-permute-done | bytes 131104 | tf_op jit(solution)/shard_map/ppermute | solution.py:14
  126.7 3.5 %gather_fusion.7 = f32[1024,256]{1,0:T(8,128)S(1)} fusion(f32[512,256]{1,0:T(8,128)S(1)} %scatter_fusion.5, s32[1024]{0:T(1024)S(1)} %broadcast_clamp_fusion), kind=kCustom, calls=%fused_computation.7 | custom fusion | bytes 2101248 | tf_op jit(solution)/shard_map/gather | solution.py:139
  131.4 3.5 %all-to-all-start.2 = ((f32[32,32,256]{2,1,0:T(8,128)}), f32[32,32,256]{2,1,0:T(8,128)S(1)}, u32[]{:S(2)}, u32[]{:S(2)}) async-start(f32[32,32,256]{2,1,0:T(8,128)} %broadcast_multiply_fusion), calls=%async_computation.2 | async-start | bytes 2097152 | tf_op jit(solution)/shard_map/all_to_all | solution.py:140
  135.0 1.9 fusion.8
  136.9 35.2 %all-reduce.3.cloned.1.call-done = f32[256,256]{1,0:T(8,128)} async-done(((f32[256,256]{1,0:T(8,128)}), f32[256,256]{1,0:T(8,128)}) %all-reduce.3.cloned.1.call-update) | async-done | bytes 262160 | tf_op jit(solution)/shard_map/psum | solution.py:131
  172.2 5.8 %psum.30 = f32[256]{0:T(256)S(1)} all-reduce(f32[256]{0:T(256)S(1)} %get-tuple-element.6), channel_id=1, replica_groups=mesh['row'=8,'col'=4] {'col'}, use_global_device_ids=true, to_apply=%region_18.19 | all-reduce | flops 256 | bytes 2048 | tf_op jit(solution)/shard_map/psum | solution.py:131
  177.9 21.4 %psum.31 = f32[256]{0:T(256)S(1)} all-reduce(f32[256]{0:T(256)S(1)} %psum.30), channel_id=1, replica_groups=mesh['row'=8,'col'=4] {'row'}, use_global_device_ids=true, to_apply=%region_19.20 | all-reduce | flops 256 | bytes 2048 | tf_op jit(solution)/shard_map/psum | solution.py:131
  199.9 46.6 %all-reduce.5.cloned.1.call-done = f32[256,256]{1,0:T(8,128)} async-done(((f32[256,256]{1,0:T(8,128)}), f32[256,256]{1,0:T(8,128)}) %all-reduce.5.cloned.1.call-update) | async-done | bytes 262160 | tf_op jit(solution)/shard_map/psum | solution.py:131
  248.2 2.2 gather_fusion.8
  (105 shorter events, 34.5 us)
Async XLA Ops:
  7.2 99.1 %copy-start = (f32[256,256]{1,0:T(8,128)S(1)}, f32[256,256]{1,0:T(8,128)}, u32[]{:S(2)}) copy-start(f32[256,256]{1,0:T(8,128)} %param.12) | copy-start | bytes 786436
  42.9 14.4 %all-to-all-start = ((s32[32,1,32]{2,1,0:T(1,128)}), s32[32,1,32]{2,1,0:T(1,128)S(1)}, u32[]{:S(2)}, u32[]{:S(2)}) async-start(s32[32,1,32]{2,1,0:T(1,128)} %all_to_all.12), calls=%async_computation | async-start | bytes 32768 | tf_op jit(solution)/shard_map/all_to_all | solution.py:115
  57.2 2.8 %copy-start.6 = (s32[1,3]{1,0:T(1,128)S(1)}, s32[1,3]{1,0:T(1,128)}, u32[]{:S(2)}) copy-start(s32[1,3]{1,0:T(1,128)} %param.16) | copy-start | bytes 40
  57.3 29.0 %all-to-all-start.1 = ((f32[32,32,256]{2,1,0:T(8,128)}), f32[32,32,256]{2,1,0:T(8,128)S(1)}, u32[]{:S(2)}, u32[]{:S(2)}) async-start(f32[32,32,256]{2,1,0:T(8,128)} %bitcast.36), calls=%async_computation.1 | async-start | bytes 2097152 | tf_op jit(solution)/shard_map/all_to_all | solution.py:108
  62.6 0.7 copy-start.7
  63.3 0.7 copy-start.8
  91.2 1.0 copy-start.1
  95.6 2.5 collective-permute-start
  96.6 1.6 copy-start.3
  96.6 6.0 %collective-permute-start.1 = (f32[128,256]{0,1:T(8,128)S(1)}, f32[128,256]{0,1:T(8,128)S(1)}, u32[]{:S(2)}, u32[]{:S(2)}) collective-permute-start(f32[128,256]{0,1:T(8,128)S(1)} %broadcast_multiply_fusion.3), channel_id=1, source_target_pairs={{0,2},{1,3},{2,0},{3,1},{4,6},{5,7},{6,4},{7,5},{8,10},{9,11},{10,... | collective-permute-start | bytes 393224 | tf_op jit(solution)/shard_map/ppermute | solution.py:14
  106.3 0.7 copy-start.9
  107.0 1.5 copy-start.4
  108.4 0.8 copy-start.10
  111.0 1.0 copy-start.2
  114.2 2.5 copy-start.5
  117.2 2.0 collective-permute-start.2
  117.6 6.0 %collective-permute-start.3 = (f32[128,256]{0,1:T(8,128)S(1)}, f32[128,256]{0,1:T(8,128)S(1)}, u32[]{:S(2)}, u32[]{:S(2)}) collective-permute-start(f32[128,256]{0,1:T(8,128)S(1)} %convolution_bitcast_fusion), channel_id=1, source_target_pairs={{0,2},{1,3},{2,0},{3,1},{4,6},{5,7},{6,4},{7,5},{8,10},{9,11},{10,... | collective-permute-start | bytes 393224 | tf_op jit(solution)/shard_map/ppermute | solution.py:14
  131.4 3.6 %copy-start.11 = (f32[512,256]{1,0:T(8,128)S(1)}, f32[512,256]{1,0:T(8,128)}, u32[]{:S(2)}) copy-start(f32[512,256]{1,0:T(8,128)} %copy-done.10) | copy-start | bytes 1572868
  131.4 116.8 %all-to-all-start.2 = ((f32[32,32,256]{2,1,0:T(8,128)}), f32[32,32,256]{2,1,0:T(8,128)S(1)}, u32[]{:S(2)}, u32[]{:S(2)}) async-start(f32[32,32,256]{2,1,0:T(8,128)} %broadcast_multiply_fusion), calls=%async_computation.2 | async-start | bytes 2097152 | tf_op jit(solution)/shard_map/all_to_all | solution.py:140
  134.9 37.2 %all-reduce.3.cloned.1.call-start = ((), (), s32[]{:S(2)}) async-start(), calls=%async_computation.3 | async-start | bytes 524288 | tf_op jit(solution)/shard_map/psum | solution.py:131
  136.9 109.6 %all-reduce.5.cloned.1.call-start = ((), (), s32[]{:S(2)}) async-start(), calls=%async_computation.4 | async-start | bytes 524288 | tf_op jit(solution)/shard_map/psum | solution.py:131
Sparse Core Ops, SparseCore 0:
  138.7 33.4 all-reduce.2
  175.8 70.5 all-reduce.4
